TPU v7x, 256 devices: a whole 4x4x8 slice. The times are simulated.
256 devices in a mesh: dp: 4 (over x), seq: 4 (over y_hi, core), tensor: 16 (over y_lo, z).
Axes of the slice: x: 4, y: 4 (y_hi: 2, y_lo: 2; y = y_hi * 2 + y_lo), z: 8, core: 2. Of those that a mesh axis runs over, the one named last changes fastest.
Arguments:
- byte_acts: bfloat16 [4, 16384, 2048], P('dp', 'seq', 'tensor'), may hold values from -18 to 18
- conv_weight: bfloat16 [16, 1024, 128], P('tensor'), may hold values from -0.1875 to 0.1875
- conv_bias: float32 [2048], P('tensor'), may hold values from -3 to 3
- proj_weight: bfloat16 [2048, 8192], P(None, 'tensor'), may hold values from -0.125 to 0.125
- teacher: bfloat16 [4, 4096, 8192], P('dp', 'seq', 'tensor'), may hold values from -6 to 6
- span_lengths: int32 [4, 4096], P('dp'), may hold values from 1 to 16, as said below
Outputs:
- downsampled: bfloat16 [4, 4096, 2048], P('dp', 'seq', 'tensor')
- byte_grad: bfloat16 [4, 16384, 2048], P('dp', 'seq', 'tensor')
- conv_grad: float32 [16, 1024, 128], P('tensor')
- proj_grad: float32 [2048, 8192], P(None, 'tensor')
Inputs may be any that keep to these rules, and one draw needn't show every extreme that they name: `span_lengths`: each document's 4096 span lengths cover its 16384 bytes in order; the longest is exactly 16.
All inputs are finite; a program needn't handle non-finite values.
Results may differ from a plain program's by a relative error of at most 0.019.
Values may be sent and summed in bfloat16 or wider, within the bound.
No kernel may reach another device: no remote copies, remote signals or barrier semaphores. Data moves between devices by JAX's collectives and lax.ppermute only.
A program may use at most 64 MiB of HBM per device.

v0:
```python
import jax
import jax.numpy as jnp
from jax import lax
from jax.sharding import PartitionSpec as P

STRIDE = 4
KERNEL = 8


def shifted(block, axis, distance):
    devices = range(lax.axis_size(axis))
    route = [(i - distance, i) for i in devices if i - distance in devices]
    return lax.ppermute(block, axis, route)


def intersection_weights(span_start, span_end, span_lengths, first_position, position_count):
    byte_first = (first_position + jnp.arange(position_count, dtype=jnp.int32)) * STRIDE
    lower_edge = jnp.maximum(span_start[:, None], byte_first[None, :])
    upper_edge = jnp.minimum(span_end[:, None], byte_first[None, :] + STRIDE)
    covered = jnp.maximum(upper_edge - lower_edge, 0).astype(jnp.float32)
    return (covered / span_lengths[:, None].astype(jnp.float32)).astype(jnp.bfloat16)


def local(byte_acts, conv_weight, conv_bias, proj_weight, teacher, span_lengths):
    byte_rows = byte_acts[0]
    row_total, width = byte_rows.shape
    groups_here = conv_weight.shape[0]
    group_width = width // groups_here
    positions = row_total // STRIDE
    seq_count = lax.axis_size("seq")
    seq_rank = lax.axis_index("seq")
    lengths_doc = span_lengths[0]
    tokens_all = lengths_doc.shape[0]
    span_end = jnp.cumsum(lengths_doc)
    span_start = span_end - lengths_doc
    next_rows = shifted(byte_rows[:STRIDE], "seq", -1)
    extended = jnp.concatenate([byte_rows, next_rows], axis=0)
    blocks = extended.reshape(positions + 1, STRIDE, groups_here, group_width)
    windows = jnp.concatenate([blocks[:-1], blocks[1:]], axis=1)
    taps_weight = conv_weight.reshape(groups_here, KERNEL, group_width, group_width)
    conv_out = jnp.einsum(
        "pkgc,gkco->pgo", windows, taps_weight, preferred_element_type=jnp.float32
    )
    conv_out = conv_out + conv_bias.reshape(groups_here, group_width)[None]
    downsampled = conv_out.reshape(positions, width).astype(jnp.bfloat16)
    local_weight = intersection_weights(
        span_start, span_end, lengths_doc, seq_rank * positions, positions
    )
    weight_part = local_weight
    pooled_sum = lax.psum_scatter(
        jnp.dot(weight_part, downsampled, preferred_element_type=jnp.float32).astype(jnp.bfloat16),
        "seq",
        scatter_dimension=0,
        tiled=True,
    )
    gathered = lax.all_gather(pooled_sum, "tensor", axis=1, tiled=True)
    predicted = jnp.dot(gathered, proj_weight, preferred_element_type=jnp.float32)
    err_grad = (predicted - teacher[0].astype(jnp.float32)).astype(jnp.bfloat16)
    proj_local = lax.dot_general(
        gathered, err_grad, (((0,), (0,)), ((), ())), preferred_element_type=jnp.float32
    )
    token_scale = 1.0 / jnp.sqrt(jnp.float32(lax.axis_size("dp") * tokens_all))
    proj_summed = lax.psum(proj_local.astype(jnp.bfloat16), ("dp", "seq")).astype(jnp.float32)
    proj_grad = proj_summed * token_scale
    weight_part = proj_weight
    pooled_grad_t = lax.psum_scatter(
        lax.dot_general(
            weight_part, err_grad, (((1,), (1,)), ((), ())), preferred_element_type=jnp.float32
        ).astype(jnp.bfloat16),
        "tensor",
        scatter_dimension=0,
        tiled=True,
    )
    weight_part = local_weight
    down_sum = lax.dot_general(
        weight_part,
        lax.all_gather(pooled_grad_t, "seq", axis=1, tiled=True),
        (((0,), (1,)), ((), ())),
        preferred_element_type=jnp.float32,
    )
    down_grad = down_sum.astype(jnp.bfloat16).reshape(positions, groups_here, group_width)
    conv_local = jnp.einsum(
        "pkgc,pgo->gkco", windows, down_grad, preferred_element_type=jnp.float32
    )
    conv_summed = lax.psum(conv_local.astype(jnp.bfloat16), ("dp", "seq")).astype(jnp.float32)
    position_scale = 1.0 / jnp.sqrt(jnp.float32(lax.axis_size("dp") * positions * seq_count))
    conv_grad = (conv_summed * position_scale).reshape(
        groups_here, KERNEL * group_width, group_width
    )
    window_grad = jnp.einsum(
        "pgo,gkco->pkgc", down_grad, taps_weight, preferred_element_type=jnp.float32
    )
    incoming = shifted(window_grad[-1, STRIDE:], "seq", 1)
    carried_grad = jnp.concatenate([incoming[None], window_grad[:-1, STRIDE:]], axis=0)
    byte_grad = (
        (window_grad[:, :STRIDE] + carried_grad).reshape(row_total, width).astype(jnp.bfloat16)
    )
    return (downsampled[None], byte_grad[None], conv_grad, proj_grad)


def solution(mesh):
    return jax.shard_map(
        local,
        mesh=mesh,
        in_specs=(
            P("dp", "seq", "tensor"),
            P("tensor", None, None),
            P("tensor"),
            P(None, "tensor"),
            P("dp", "seq", "tensor"),
            P("dp", None),
        ),
        out_specs=(
            P("dp", "seq", "tensor"),
            P("dp", "seq", "tensor"),
            P("tensor", None, None),
            P(None, "tensor"),
        ),
        check_vma=False,
    )
```

profile of v0, /device:TPU:1, one launch (start us, length us, event | category | flops | bytes accessed | tf_op | source)
XLA Modules:
  0.0 448.6 jit_solution(9548664783384587583)
XLA Ops:
  8.1 5.1 %collective-permute-start = (bf16[4,128]{1,0:T(4,128)(2,1)S(1)}, bf16[4,128]{1,0:T(4,128)(2,1)S(1)}, u32[]{:S(2)}, u32[]{:S(2)}) collective-permute-start(bf16[4,128]{1,0:T(4,128)(2,1)S(1)} %slice_bitcast_fusion), channel_id=1, source_target_pairs={{16,0},{32,16},{48,32},{17,1},{33,17},{49,33},{18,2},{34,18},{50,3... | collective-permute-start | bytes 3080 | tf_op jit(solution)/shard_map/ppermute | solution.py:13
  13.2 1.0 reduce-window.9
  16.0 1.4 copy.17
  17.4 1.5 pad_maximum_fusion
  19.1 1.0 copy-done.1
  21.5 7.5 %fusion.2 = bf16[4096,128]{1,0:T(8,128)(2,1)} fusion(f32[4096]{0:T(1024)S(1)} %convert_element_type.87, s32[1024]{0:T(1024)S(1)} %add_multiply_fusion, s32[4096]{0:T(1024)S(1)} %get-tuple-element.6, s32[1024]{0:T(1024)S(1)} %broadcast_add_fusion, s32[4096]{0:T(1024)S(1)} %get-tuple-element.7, bf16[1,128,1024]{1,2,0:T(8,128)(2,1)S(1)} %fusion.11), kind=kOutput, calls=%fused_computation.3 | convolution fusion | flops 1103626240 | bytes 1368064 | tf_op jit(solution)/shard_map/dot_general | solution.py:51
  29.0 38.1 %reduce-scatter.5.cloned.1.call-done = bf16[1024,128]{1,0:T(8,128)(2,1)} async-done(((bf16[4096,128]{1,0:T(8,128)(2,1)}), bf16[1024,128]{1,0:T(8,128)(2,1)}) %reduce-scatter.5.cloned.1.call-update) | async-done | bytes 262160 | tf_op jit(solution)/shard_map/reduce_scatter | solution.py:50
  67.2 80.8 %all-gather.3.cloned.1.call-done = bf16[1024,2048]{1,0:T(8,128)(2,1)} async-done(((bf16[1024,128]{1,0:T(8,128)(2,1)}), bf16[1024,2048]{1,0:T(8,128)(2,1)}) %all-gather.3.cloned.1.call-update) | async-done | bytes 4194320 | tf_op jit(solution)/shard_map/all_gather | solution.py:56
  148.1 4.6 %fusion.24 = f32[1024,512]{1,0:T(8,128)S(1)} fusion(bf16[1024,2048]{1,0:T(8,128)(2,1)} %all-gather.3.cloned.1.call-done, bf16[2048,512]{1,0:T(8,128)(2,1)S(1)} %copy-done), kind=kOutput, calls=%fused_computation.37 | convolution fusion | flops 2147483648 | bytes 8388608 | tf_op jit(solution)/shard_map/dot_general | solution.py:57
  152.7 1.4 copy-done.8
  154.0 4.4 convert_bitcast_fusion
  158.4 6.4 %copy.23 = bf16[2048,1024]{1,0:T(8,128)(2,1)} copy(bf16[2048,1024]{0,1:T(8,128)(2,1)} %convert_bitcast_fusion) | data formatting | bytes 8388608
  164.9 78.6 %reduce-scatter.7.cloned.1.call-done = bf16[128,1024]{1,0:T(8,128)(2,1)} async-done(((bf16[2048,1024]{1,0:T(8,128)(2,1)}), bf16[128,1024]{1,0:T(8,128)(2,1)}) %reduce-scatter.7.cloned.1.call-update) | async-done | bytes 262160
  243.5 1.8 copy.24
  245.6 6.8 %convolution_convert_fusion = bf16[2048,512]{1,0:T(8,128)(2,1)} fusion(bf16[1024,2048]{1,0:T(8,128)(2,1)} %all-gather.3.cloned.1.call-done, f32[1024,512]{1,0:T(8,128)} %copy-done.8, bf16[1,1024,512]{2,1,0:T(8,128)(2,1)} %param.10), kind=kOutput, calls=%fused_computation.6 | convolution fusion | flops 2150105088 | bytes 9437184 | tf_op jit(solution)/shard_map/dot_general | solution.py:59
  252.3 24.2 %all-gather.5.cloned.1.call-done = bf16[128,4096]{0,1:T(8,128)(2,1)} async-done(((bf16[128,1024]{0,1:T(8,128)(2,1)}), bf16[128,4096]{0,1:T(8,128)(2,1)}) %all-gather.5.cloned.1.call-update) | async-done | bytes 1048592 | tf_op jit(solution)/shard_map/all_gather | solution.py:77
  276.5 7.7 %fusion.15 = bf16[1024,128,1]{1,0,2:T(8,128)(2,1)S(1)} fusion(bf16[128,4096]{0,1:T(8,128)(2,1)} %all-gather.5.cloned.1.call-done, f32[4096]{0:T(1024)S(1)} %convert_element_type.87, s32[1024]{0:T(1024)S(1)} %add_multiply_fusion, s32[4096]{0:T(1024)S(1)} %get-tuple-element.6, s32[1024]{0:T(1024)S(1)} %broadcast_add_fusion, s32[4096]{0:T(1024)S(1)} %get-tuple-element.7), kind=kOutput, calls=%fused_computation.21 | convolution fusion | flops 1103233024 | bytes 1368064 | tf_op jit(solution)/shard_map/dot_general | solution.py:75
  284.9 1.4 fusion.14
  286.4 1.7 convolution_bitcast_fusion
  288.1 2.1 collective-permute-start.1
  291.4 1.8 copy.20
  293.2 142.9 %all-reduce.3.cloned.1.call-done = (bf16[1,8,128,128]{3,2,1,0:T(8,128)(2,1)}, bf16[2048,512]{1,0:T(8,128)(2,1)}) async-done(((bf16[1,8,128,128]{3,2,1,0:T(8,128)(2,1)}, bf16[2048,512]{1,0:T(8,128)(2,1)}), (bf16[1,8,128,128]{3,2,1,0:T(8,128)(2,1)}, bf16[2048,512]{1,0:T(8,128)(2,1)})) %all-reduce.3.cloned.1.call-update) | async-done | bytes 2359312 | tf_op jit(solution)/shard_map/psum | solution.py:85
  436.1 1.8 convert_multiply_fusion.1
  437.9 4.2 convert_multiply_fusion
  (41 shorter events, 6.6 us)
Async XLA Ops:
  7.2 140.9 %copy-start = (bf16[2048,512]{1,0:T(8,128)(2,1)S(1)}, bf16[2048,512]{1,0:T(8,128)(2,1)}, u32[]{:S(2)}) copy-start(bf16[2048,512]{1,0:T(8,128)(2,1)} %param.9) | copy-start | bytes 6291460
  7.2 12.8 %copy-start.6 = (f32[128]{0:T(128)S(1)}, f32[128]{0:T(128)}, u32[]{:S(2)}) copy-start(f32[128]{0:T(128)} %param.8) | copy-start | bytes 1540
  7.2 12.8 %copy-start.3 = (bf16[1,1024,128]{2,1,0:T(8,128)(2,1)S(1)}, bf16[1,1024,128]{2,1,0:T(8,128)(2,1)}, u32[]{:S(2)}) copy-start(bf16[1,1024,128]{2,1,0:T(8,128)(2,1)} %param.7) | copy-start | bytes 786436
  7.2 60.0 %reduce-scatter.5.cloned.1.call-start = ((), (), s32[]{:S(2)}) async-start(), calls=%async_computation.2 | async-start | bytes 1310720 | tf_op jit(solution)/shard_map/reduce_scatter | solution.py:50
  8.1 9.3 %collective-permute-start = (bf16[4,128]{1,0:T(4,128)(2,1)S(1)}, bf16[4,128]{1,0:T(4,128)(2,1)S(1)}, u32[]{:S(2)}, u32[]{:S(2)}) collective-permute-start(bf16[4,128]{1,0:T(4,128)(2,1)S(1)} %slice_bitcast_fusion), channel_id=1, source_target_pairs={{16,0},{32,16},{48,32},{17,1},{33,17},{49,33},{18,2},{34,18},{50,3... | collective-permute-start | bytes 3080 | tf_op jit(solution)/shard_map/ppermute | solution.py:13
  19.0 1.0 copy-start.1
  20.7 0.7 copy-start.7
  29.0 119.1 %all-gather.3.cloned.1.call-start = ((), (), s32[]{:S(2)}) async-start(), calls=%async_computation.3 | async-start | bytes 4456448 | tf_op jit(solution)/shard_map/all_gather | solution.py:56
  67.2 176.3 %reduce-scatter.7.cloned.1.call-start = ((), (), s32[]{:S(2)}) async-start(), calls=%async_computation.5 | async-start | bytes 4456448
  148.1 6.0 %copy-start.5 = (bf16[1,1024,512]{2,1,0:T(8,128)(2,1)S(1)}, bf16[1,1024,512]{2,1,0:T(8,128)(2,1)}, u32[]{:S(2)}) copy-start(bf16[1,1024,512]{2,1,0:T(8,128)(2,1)} %param.10) | copy-start | bytes 3145732
  152.7 1.4 copy-start.8
  164.9 111.6 %all-gather.5.cloned.1.call-start = ((), (), s32[]{:S(2)}) async-start(), calls=%async_computation.4 | async-start | bytes 1310720 | tf_op jit(solution)/shard_map/all_gather | solution.py:77
  245.3 190.8 %all-reduce.3.cloned.1.call-start = ((), (), s32[]{:S(2)}) async-start(), calls=%async_computation.6 | async-start | bytes 4718592 | tf_op jit(solution)/shard_map/psum | solution.py:85
  276.5 8.4 %copy-start.2 = (bf16[1024,4,1,128]{3,0,1,2:T(8,128)(2,1)S(1)}, bf16[1024,4,1,128]{3,0,1,2:T(8,128)(2,1)}, u32[]{:S(2)}) copy-start(bf16[1024,4,1,128]{3,0,1,2:T(8,128)(2,1)} %copy-done.1) | copy-start | bytes 3145732
  284.2 0.7 copy-start.4
  288.1 3.1 collective-permute-start.1
Sparse Core Ops, SparseCore 0:
  29.1 38.0 reduce-scatter.4
  69.0 79.0 all-gather.2
  165.0 78.4 reduce-scatter.6
  245.9 30.5 all-gather.4
  286.5 149.5 all-reduce.2
where the time goes:
time: 449 us
  waiting for transfers between devices  366 us (82%)
  matrix products  34.8 us (8%)
  local copies, waits for them, and re-layouts  16.4 us (4%)
  between operations  13.9 us (3%)
  other arithmetic  10.3 us (2%)
  starting transfers between devices  7.58 us (2%)
    psum x1, waiting for transfers between devices, local(): lax.psum(conv_local.astype(jnp.bfloat16), ('dp', 'seq')).astype(jnp.float32)  143 us
    all_gather x1, waiting for transfers between devices, local(): gathered = lax.all_gather(pooled_sum, 'tensor', axis=1, tiled=True)  80.8 us
    unnamed x6, waiting for transfers between devices  78.7 us
    reduce_scatter x1, waiting for transfers between devices, local(): lax.psum_scatter(jnp.dot(weight_part, downsampled, preferred_element_type...  38.1 us
    all_gather x1, waiting for transfers between devices, local(): lax.all_gather(pooled_grad_t, 'seq', axis=1, tiled=True)  24.2 us
    unnamed x20, local copies, waits for them, and re-layouts  12 us
  transfers between devices with their start and end apart: 7, of which 6 were waited for; matrix products, arithmetic and copies ran while one was open for 3% of the time, Pallas kernels for 0%

commit v1 on v0

--- a/solution.py
+++ b/solution.py
@@ -82,7 +82,9 @@
     conv_local = jnp.einsum(
         "pkgc,pgo->gkco", windows, down_grad, preferred_element_type=jnp.float32
     )
-    conv_summed = lax.psum(conv_local.astype(jnp.bfloat16), ("dp", "seq")).astype(jnp.float32)
+    conv_summed = lax.psum(lax.psum(conv_local.astype(jnp.bfloat16), "seq"), "dp").astype(
+        jnp.float32
+    )
     position_scale = 1.0 / jnp.sqrt(jnp.float32(lax.axis_size("dp") * positions * seq_count))
     conv_grad = (conv_summed * position_scale).reshape(
         groups_here, KERNEL * group_width, group_width

time: 449 us -> 536 us (1.19)
  waiting for transfers between devices: 366 us -> 447 us
    psum x1 -> x3, waiting for transfers between devices: 143 us -> 224 us  [the longest x1 138 us: local(): lax.psum(proj_local.astype(jnp.bfloat16), ('dp', 'seq')).astype(jnp.float32)]
    unnamed x20 -> x22, local copies, waits for them, and re-layouts: 12 us -> 13.2 us
    unnamed x6 -> x8, waiting for transfers between devices: 78.7 us -> 78.6 us
  transfers between devices with their start and end apart: 7 -> 9, of which waited for: 6 -> 7; matrix products, arithmetic and copies ran while one was open for 3% -> 6% of each run, Pallas kernels for 0% -> 0%
where the time goes in v1:
time: 536 us; the launch traced here: 534 us
  waiting for transfers between devices  447 us (83%)
  matrix products  33.7 us (6%)
  local copies, waits for them, and re-layouts  19 us (4%)
  between operations  14.3 us (3%)
  other arithmetic  12.7 us (2%)
  starting transfers between devices  7.66 us (1%)
    psum x1, waiting for transfers between devices, local(): lax.psum(proj_local.astype(jnp.bfloat16), ('dp', 'seq')).astype(jnp.float32)  138 us
    all_gather x1, waiting for transfers between devices, local(): gathered = lax.all_gather(pooled_sum, 'tensor', axis=1, tiled=True)  80.8 us
    unnamed x8, waiting for transfers between devices  78.6 us
    psum x1, waiting for transfers between devices, local(): lax.psum(conv_local.astype(jnp.bfloat16), 'seq')  45.1 us
    psum x1, waiting for transfers between devices, local(): lax.psum(lax.psum(conv_local.astype(jnp.bfloat16), 'seq'), 'dp')  41.6 us
    reduce_scatter x1, waiting for transfers between devices, local(): lax.psum_scatter(jnp.dot(weight_part, downsampled, preferred_element_type...  38.1 us
    all_gather x1, waiting for transfers between devices, local(): lax.all_gather(pooled_grad_t, 'seq', axis=1, tiled=True)  24.6 us
    unnamed x22, local copies, waits for them, and re-layouts  13.2 us
  transfers between devices with their start and end apart: 9, of which 7 were waited for; matrix products, arithmetic and copies ran while one was open for 6% of the time, Pallas kernels for 0%

profile of v1, /device:TPU:1, one launch (start us, length us, event | category | flops | bytes accessed | tf_op | source)
XLA Modules:
  0.0 533.9 jit_solution(10340372007217103008)
XLA Ops:
  8.1 5.1 collective-permute-start
  17.4 1.5 pad_maximum_fusion
  21.5 7.5 %fusion.2 = bf16[4096,128]{1,0:T(8,128)(2,1)} fusion(f32[4096]{0:T(1024)S(1)} %convert_element_type.87, s32[1024]{0:T(1024)S(1)} %add_multiply_fusion, s32[4096]{0:T(1024)S(1)} %get-tuple-element.4, s32[1024]{0:T(1024)S(1)} %broadcast_add_fusion, s32[4096]{0:T(1024)S(1)} %get-tuple-element.5, bf16[1,128,1024]{1,2,0:T(8,128)(2,1)S(1)} %fusion.11), kind=kOutput, calls=%fused_computation.3 | convolution fusion | flops 1103626240 | bytes 1368064 | tf_op jit(solution)/shard_map/dot_general | solution.py:51
  29.1 38.1 %reduce-scatter.5.cloned.1.call-done = bf16[1024,128]{1,0:T(8,128)(2,1)} async-done(((bf16[4096,128]{1,0:T(8,128)(2,1)}), bf16[1024,128]{1,0:T(8,128)(2,1)}) %reduce-scatter.5.cloned.1.call-update) | async-done | bytes 262160 | tf_op jit(solution)/shard_map/reduce_scatter | solution.py:50
  67.3 80.8 %all-gather.3.cloned.1.call-done = bf16[1024,2048]{1,0:T(8,128)(2,1)} async-done(((bf16[1024,128]{1,0:T(8,128)(2,1)}), bf16[1024,2048]{1,0:T(8,128)(2,1)}) %all-gather.3.cloned.1.call-update) | async-done | bytes 4194320 | tf_op jit(solution)/shard_map/all_gather | solution.py:56
  148.1 4.6 fusion.24
  154.0 4.4 convert_bitcast_fusion
  158.4 6.4 %copy.23 = bf16[2048,1024]{1,0:T(8,128)(2,1)} copy(bf16[2048,1024]{0,1:T(8,128)(2,1)} %convert_bitcast_fusion) | data formatting | bytes 8388608
  164.9 78.5 %reduce-scatter.7.cloned.1.call-done = bf16[128,1024]{1,0:T(8,128)(2,1)} async-done(((bf16[2048,1024]{1,0:T(8,128)(2,1)}), bf16[128,1024]{1,0:T(8,128)(2,1)}) %reduce-scatter.7.cloned.1.call-update) | async-done | bytes 262160
  243.4 1.8 copy.24
  245.3 6.8 %convolution_convert_fusion = bf16[2048,512]{1,0:T(8,128)(2,1)} fusion(bf16[1024,2048]{1,0:T(8,128)(2,1)} %all-gather.3.cloned.1.call-done, f32[1024,512]{1,0:T(8,128)} %copy-done.9, bf16[1,1024,512]{2,1,0:T(8,128)(2,1)} %param.10), kind=kOutput, calls=%fused_computation.6 | convolution fusion | flops 2150105088 | bytes 9437184 | tf_op jit(solution)/shard_map/dot_general | solution.py:59
  252.3 24.6 %all-gather.5.cloned.1.call-done = bf16[128,4096]{0,1:T(8,128)(2,1)} async-done(((bf16[128,1024]{0,1:T(8,128)(2,1)}), bf16[128,4096]{0,1:T(8,128)(2,1)}) %all-gather.5.cloned.1.call-update) | async-done | bytes 1048592 | tf_op jit(solution)/shard_map/all_gather | solution.py:77
  276.9 7.6 %fusion.15 = bf16[1024,128,1]{1,0,2:T(8,128)(2,1)S(1)} fusion(bf16[128,4096]{0,1:T(8,128)(2,1)} %all-gather.5.cloned.1.call-done, f32[4096]{0:T(1024)S(1)} %convert_element_type.87, s32[1024]{0:T(1024)S(1)} %add_multiply_fusion, s32[4096]{0:T(1024)S(1)} %get-tuple-element.4, s32[1024]{0:T(1024)S(1)} %broadcast_add_fusion, s32[4096]{0:T(1024)S(1)} %get-tuple-element.5), kind=kOutput, calls=%fused_computation.21 | convolution fusion | flops 1103233024 | bytes 1368064 | tf_op jit(solution)/shard_map/dot_general | solution.py:75
  285.2 1.9 copy-done.1
  287.2 2.1 collective-permute-start.1
  289.2 1.5 fusion.14
  290.8 137.6 %all-reduce.8.cloned.1.call-done = bf16[2048,512]{1,0:T(8,128)(2,1)} async-done(((bf16[2048,512]{1,0:T(8,128)(2,1)}), bf16[2048,512]{1,0:T(8,128)(2,1)}) %all-reduce.8.cloned.1.call-update) | async-done | bytes 2097168 | tf_op jit(solution)/shard_map/psum | solution.py:63
  428.4 4.3 convert_multiply_fusion
  432.8 1.5 slice.46
  434.2 45.1 %all-reduce.4.cloned.1.call-done = bf16[1,8,128,128]{3,2,1,0:T(8,128)(2,1)} async-done(((bf16[1,8,128,128]{3,2,1,0:T(8,128)(2,1)}), bf16[1,8,128,128]{3,2,1,0:T(8,128)(2,1)}) %all-reduce.4.cloned.1.call-update) | async-done | bytes 262160 | tf_op jit(solution)/shard_map/psum | solution.py:85
  479.4 2.5 fusion.3
  481.9 1.8 copy.20
  483.7 41.6 %all-reduce.6.cloned.1.call-done = bf16[1,8,128,128]{3,2,1,0:T(8,128)(2,1)} async-done(((bf16[1,8,128,128]{3,2,1,0:T(8,128)(2,1)}), bf16[1,8,128,128]{3,2,1,0:T(8,128)(2,1)}) %all-reduce.6.cloned.1.call-update) | async-done | bytes 262160 | tf_op jit(solution)/shard_map/psum | solution.py:85
  525.3 1.8 convert_multiply_fusion.1
  (49 shorter events, 10.2 us)
Async XLA Ops:
  7.2 140.9 %copy-start = (bf16[2048,512]{1,0:T(8,128)(2,1)S(1)}, bf16[2048,512]{1,0:T(8,128)(2,1)}, u32[]{:S(2)}) copy-start(bf16[2048,512]{1,0:T(8,128)(2,1)} %param.9) | copy-start | bytes 6291460
  7.2 12.9 %copy-start.7 = (f32[128]{0:T(128)S(1)}, f32[128]{0:T(128)}, u32[]{:S(2)}) copy-start(f32[128]{0:T(128)} %param.8) | copy-start | bytes 1540
  7.2 12.8 %copy-start.5 = (bf16[1,1024,128]{2,1,0:T(8,128)(2,1)S(1)}, bf16[1,1024,128]{2,1,0:T(8,128)(2,1)}, u32[]{:S(2)}) copy-start(bf16[1,1024,128]{2,1,0:T(8,128)(2,1)} %param.7) | copy-start | bytes 786436
  7.2 60.0 %reduce-scatter.5.cloned.1.call-start = ((), (), s32[]{:S(2)}) async-start(), calls=%async_computation.2 | async-start | bytes 1310720 | tf_op jit(solution)/shard_map/reduce_scatter | solution.py:50
  8.1 9.3 %collective-permute-start = (bf16[4,128]{1,0:T(4,128)(2,1)S(1)}, bf16[4,128]{1,0:T(4,128)(2,1)S(1)}, u32[]{:S(2)}, u32[]{:S(2)}) collective-permute-start(bf16[4,128]{1,0:T(4,128)(2,1)S(1)} %slice_bitcast_fusion), channel_id=1, source_target_pairs={{16,0},{32,16},{48,32},{17,1},{33,17},{49,33},{18,2},{34,18},{50,3... | collective-permute-start | bytes 3080 | tf_op jit(solution)/shard_map/ppermute | solution.py:13
  19.0 1.0 copy-start.3
  20.8 0.7 copy-start.8
  29.0 119.1 %all-gather.3.cloned.1.call-start = ((), (), s32[]{:S(2)}) async-start(), calls=%async_computation.3 | async-start | bytes 4456448 | tf_op jit(solution)/shard_map/all_gather | solution.py:56
  67.2 176.2 %reduce-scatter.7.cloned.1.call-start = ((), (), s32[]{:S(2)}) async-start(), calls=%async_computation.8 | async-start | bytes 4456448
  148.1 6.0 %copy-start.6 = (bf16[1,1024,512]{2,1,0:T(8,128)(2,1)S(1)}, bf16[1,1024,512]{2,1,0:T(8,128)(2,1)}, u32[]{:S(2)}) copy-start(bf16[1,1024,512]{2,1,0:T(8,128)(2,1)} %param.10) | copy-start | bytes 3145732
  152.7 1.4 copy-start.9
  164.9 112.0 %all-gather.5.cloned.1.call-start = ((), (), s32[]{:S(2)}) async-start(), calls=%async_computation.4 | async-start | bytes 1310720 | tf_op jit(solution)/shard_map/all_gather | solution.py:77
  245.2 183.2 %all-reduce.8.cloned.1.call-start = ((), (), s32[]{:S(2)}) async-start(), calls=%async_computation.7 | async-start | bytes 4194304 | tf_op jit(solution)/shard_map/psum | solution.py:63
  252.1 227.3 %all-reduce.4.cloned.1.call-start = ((), (), s32[]{:S(2)}) async-start(), calls=%async_computation.5 | async-start | bytes 524288 | tf_op jit(solution)/shard_map/psum | solution.py:85
  284.5 4.7 copy-start.4
  285.2 1.9 copy-start.1
  287.2 192.2 %collective-permute-start.1 = (f32[4,1,128]{2,0,1:T(4,128)S(1)}, f32[4,1,128]{2,0,1:T(4,128)S(1)}, u32[]{:S(2)}, u32[]{:S(2)}) collective-permute-start(f32[4,1,128]{2,0,1:T(4,128)S(1)} %bitcast.91), channel_id=1, source_target_pairs={{0,16},{16,32},{32,48},{1,17},{17,33},{33,49},{2,18},{18,34},{34,5... | collective-permute-start | bytes 6152 | tf_op jit(solution)/shard_map/ppermute | solution.py:13
  290.7 234.6 %all-reduce.6.cloned.1.call-start = ((), (), s32[]{:S(2)}) async-start(), calls=%async_computation.6 | async-start | bytes 524288 | tf_op jit(solution)/shard_map/psum | solution.py:85
  428.4 4.4 copy-start.2
Sparse Core Ops, SparseCore 0:
  29.1 38.0 reduce-scatter.4
  69.0 79.0 all-gather.2
  165.0 78.3 reduce-scatter.6
  245.8 31.0 all-gather.4
  280.2 148.2 all-reduce.7
  431.7 47.6 all-reduce.3
  481.7 43.5 all-reduce.5
